TPU v7x, 32 devices: a whole 2x2x4 slice. The times are simulated.
32 devices in a mesh: dp: 4 (over x, core), fsdp: 8 (over z, y).
Axes of the slice: x: 2, y: 2, z: 4, core: 2. Of those that a mesh axis runs over, the one named last changes fastest.
Arguments:
- tokens: bfloat16 [8192, 640], P(('dp', 'fsdp')), may hold values from -6 to 6
- cotangent: bfloat16 [8192, 640], P(('dp', 'fsdp')), may hold values from -6 to 6
- masked_pos: int32 [8192], P(('dp', 'fsdp')), may hold values from 0 to 1
- labels: int32 [8192], P(('dp', 'fsdp')), may hold values from 0 to 3
- decoder: bfloat16 [4, 640], replicated, may hold values from -0.375 to 0.375
- master: float32 [640, 12800], P('fsdp'), may hold values from -0.6324555 to 0.6324555
- small_params: float32 [640, 16], P('fsdp'), may hold values from -0.8 to 1.4
- small_first: float32 [640, 16], P('fsdp'), may hold values from -128 to 128
- small_second: float32 [640, 16], P('fsdp'), may hold values from 163.84 to 4096
- block_slots: int32 [40], replicated, may hold values from 0 to 39, as said below
- first_moment: float32 [40, 640, 320], P('fsdp'), may hold values from -128 to 128
- second_moment: float32 [40, 640, 320], P('fsdp'), may hold values from 163.84 to 4096
- left_bases: float32 [40, 640, 640], P('fsdp'), may hold values from -1 to 1, as said below
- right_bases: float32 [40, 320, 320], P('fsdp'), may hold values from -1 to 1, as said below
Outputs:
- out_tokens: bfloat16 [8192, 640], P(('dp', 'fsdp'))
- grad_tokens: bfloat16 [8192, 640], P(('dp', 'fsdp'))
- grad_weights: float32 [640, 12800], P('fsdp')
- grad_small: float32 [640, 16], P('fsdp')
- new_first: float32 [40, 640, 320], P('fsdp')
- new_second: float32 [40, 640, 320], P('fsdp')
- new_master: float32 [640, 12800], P('fsdp')
- new_copy: bfloat16 [640, 12800], P('fsdp')
- new_small: float32 [640, 16], P('fsdp')
- new_small_first: float32 [640, 16], P('fsdp')
- new_small_second: float32 [640, 16], P('fsdp')
- loss_accuracy: float32 [5], replicated
- counts: int32 [4], replicated
Inputs may be any that keep to these rules, and one draw needn't show every extreme that they name: Distinct slot numbers; block b (columns b * 320 to (b + 1) * 320 - 1 of the weights) keeps its optimizer state in slot block_slots[b], held by fsdp index block_slots[b] // 5; at most 5 blocks on one index. `left_bases`: each slot's matrix is orthogonal. `right_bases`: each slot's matrix is orthogonal.
All inputs are finite; a program needn't handle non-finite values.
Results may differ from a plain program's by a relative error of at most 0.013.
The roundings to bfloat16 on the way count: a program that leaves them out, or rounds other values in their place, can miss the bound.
Values may be sent and summed in bfloat16 or wider, within the bound.
No kernel may reach another device: no remote copies, remote signals or barrier semaphores. Data moves between devices by JAX's collectives and lax.ppermute only.
A program may use at most 256 MiB of HBM per device.

v0:
```python
import jax
import jax.numpy as jnp
from jax import lax
from jax.sharding import PartitionSpec as P

HEAD_DIM = 32
SEQ_LEN = 256
STEP = 5
EPS_NORM = 1e-05
EPS_ADAM = 1e-08
BETA_FIRST = 0.5
BETA_SECOND = 0.5
RATE_MATRIX = 0.02
RATE_VECTOR = 0.05
EXACT_PRECISION = lax.Precision.HIGHEST


def normalize_layer(rows_in, norm_gain, norm_shift):
    centred = rows_in - jnp.mean(rows_in, axis=-1, keepdims=True)
    variance = jnp.mean(centred * centred, axis=-1, keepdims=True)
    return centred * lax.rsqrt(variance + EPS_NORM) * norm_gain + norm_shift


def exact_gelu(inputs):
    return jax.nn.gelu(inputs, approximate=False)


def adam_direction(first_new, second_new):
    return (
        first_new
        / (1.0 - BETA_FIRST**STEP)
        / (jnp.sqrt(second_new / (1.0 - BETA_SECOND**STEP)) + EPS_ADAM)
    )


def contract_rows(left_mat, right_mat):
    return lax.dot_general(
        left_mat, right_mat, (((0,), (0,)), ((), ())), preferred_element_type=jnp.float32
    )


def times_transpose(left_mat, right_mat):
    return lax.dot_general(
        left_mat, right_mat, (((1,), (1,)), ((), ())), preferred_element_type=jnp.float32
    )


def block_scores(queries, key_rows):
    return jnp.einsum(
        "slhd,smhd->shlm", queries, key_rows, preferred_element_type=jnp.float32
    ) * HEAD_DIM ** (-0.5)


def attend_block(weight_blocks):
    queries, key_rows, values = weight_blocks
    scores = block_scores(queries, key_rows)
    highest = jnp.max(scores, axis=-1, keepdims=True)
    exponent = jnp.exp(scores - highest)
    totals = jnp.sum(exponent, axis=-1, keepdims=True)
    weights_soft = (exponent / totals).astype(jnp.bfloat16)
    mixed_rows = jnp.einsum(
        "shlm,smhd->slhd", weights_soft, values, preferred_element_type=jnp.float32
    )
    return (mixed_rows.astype(jnp.bfloat16), (highest + jnp.log(totals))[..., 0])


def attend_back(weight_blocks):
    queries, key_rows, values, log_total, d_attended = weight_blocks
    probabilities = jnp.exp(block_scores(queries, key_rows) - log_total[..., None])
    d_values = jnp.einsum(
        "shlm,slhd->smhd",
        probabilities.astype(jnp.bfloat16),
        d_attended,
        preferred_element_type=jnp.float32,
    )
    d_probs = jnp.einsum("slhd,smhd->shlm", d_attended, values, preferred_element_type=jnp.float32)
    d_scores = (
        probabilities * (d_probs - jnp.sum(probabilities * d_probs, axis=-1, keepdims=True))
    ).astype(jnp.bfloat16)
    d_queries = jnp.einsum(
        "shlm,smhd->slhd", d_scores, key_rows, preferred_element_type=jnp.float32
    ) * HEAD_DIM ** (-0.5)
    d_keys = jnp.einsum(
        "shlm,slhd->smhd", d_scores, queries, preferred_element_type=jnp.float32
    ) * HEAD_DIM ** (-0.5)
    return (
        d_queries.astype(jnp.bfloat16),
        d_keys.astype(jnp.bfloat16),
        d_values.astype(jnp.bfloat16),
    )


def local(
    tokens,
    cotangent,
    masked_pos,
    labels,
    decoder,
    master,
    small_params,
    small_first,
    small_second,
    block_slots,
    first_moment,
    second_moment,
    left_bases,
    right_bases,
):
    model_width = decoder.shape[1]
    hidden = (master.shape[1] - 4 * model_width) // 2
    heads_count = model_width // HEAD_DIM
    token_count = tokens.shape[0]
    local_weights = master.astype(jnp.bfloat16)
    local_small = small_params.astype(jnp.bfloat16)
    weights, small_all = (
        lax.all_gather(local_weights, "fsdp", axis=0, tiled=True),
        lax.all_gather(local_small, "fsdp", axis=0, tiled=True),
    )
    params = small_all.astype(jnp.float32)
    gain_one, shift_one, bias_query, bias_value, bias_output, gain_two, shift_two, bias_down = [
        params[:, column] for column in range(8)
    ]
    bias_up = params[:, 8:].reshape(hidden)
    rows_in = tokens.astype(jnp.float32)
    normed = normalize_layer(rows_in, gain_one, shift_one).astype(jnp.bfloat16)
    bias_qkv = jnp.concatenate([bias_query, jnp.zeros_like(bias_query), bias_value])
    projected = (
        jnp.dot(normed, weights[:, : 3 * model_width], preferred_element_type=jnp.float32)
        + bias_qkv
    ).astype(jnp.bfloat16)
    seq_count = token_count // SEQ_LEN
    per_block = max(1, min(seq_count, 512 // SEQ_LEN))
    block_shape = (seq_count // per_block, per_block, SEQ_LEN, heads_count, HEAD_DIM)
    queries = projected[:, :model_width].reshape(block_shape)
    key_rows = projected[:, model_width : 2 * model_width].reshape(block_shape)
    values = projected[:, 2 * model_width :].reshape(block_shape)
    attention_result, log_total = lax.map(attend_block, (queries, key_rows, values))
    attention_result = attention_result.reshape(token_count, model_width)
    middle = (
        rows_in
        + jnp.dot(
            attention_result,
            weights[:, 3 * model_width : 4 * model_width],
            preferred_element_type=jnp.float32,
        )
        + bias_output
    )
    normed_two = normalize_layer(middle, gain_two, shift_two).astype(jnp.bfloat16)
    pre_active = (
        jnp.dot(
            normed_two,
            weights[:, 4 * model_width : 4 * model_width + hidden],
            preferred_element_type=jnp.float32,
        )
        + bias_up
    )
    active = exact_gelu(pre_active).astype(jnp.bfloat16)
    output_rows = (
        middle + times_transpose(active, weights[:, 4 * model_width + hidden :]) + bias_down
    )
    out_tokens = output_rows.astype(jnp.bfloat16)
    logits = times_transpose(out_tokens, decoder)
    log_norm = jax.nn.logsumexp(logits, axis=-1)
    one_hot = (labels[:, None] == jnp.arange(decoder.shape[0], dtype=jnp.int32)[None, :]).astype(
        jnp.float32
    )
    hidden_tokens = masked_pos.astype(jnp.float32)
    chosen = one_hot * hidden_tokens[:, None]
    entropy = log_norm - jnp.sum(one_hot * logits, axis=-1)
    right_prob = jnp.sum(one_hot * jnp.exp(logits - log_norm[:, None]), axis=-1)
    local_sums = jnp.concatenate(
        [jnp.sum(hidden_tokens * entropy)[None], jnp.sum(chosen * right_prob[:, None], axis=0)]
    )
    global_sums, global_counts = lax.psum((local_sums, jnp.sum(chosen, axis=0)), ("dp", "fsdp"))
    loss_accuracy = jnp.concatenate(
        [
            global_sums[:1] / jnp.maximum(jnp.sum(global_counts), 1.0),
            global_sums[1:] / jnp.maximum(global_counts, 1.0),
        ]
    )
    counts = global_counts.astype(jnp.int32)
    weights_back, small_back = (
        lax.all_gather(local_weights, "fsdp", axis=0, tiled=True),
        lax.all_gather(local_small, "fsdp", axis=0, tiled=True),
    )
    params_back = small_back.astype(jnp.float32)
    back_rows = cotangent.astype(jnp.float32)
    d_active = jnp.dot(
        cotangent, weights_back[:, 4 * model_width + hidden :], preferred_element_type=jnp.float32
    )
    unused, gelu_pull = jax.vjp(exact_gelu, pre_active)
    d_pre = gelu_pull(d_active)[0].astype(jnp.bfloat16)
    d_normed_two = times_transpose(
        d_pre, weights_back[:, 4 * model_width : 4 * model_width + hidden]
    )
    unused, norm_pull_two = jax.vjp(normalize_layer, middle, params_back[:, 5], params_back[:, 6])
    d_middle_norm, d_gain_two, d_shift_two = norm_pull_two(d_normed_two)
    d_middle = back_rows + d_middle_norm
    d_branch = d_middle.astype(jnp.bfloat16)
    d_attended = times_transpose(
        d_branch, weights_back[:, 3 * model_width : 4 * model_width]
    ).astype(jnp.bfloat16)
    d_queries, d_keys, d_values = lax.map(
        attend_back, (queries, key_rows, values, log_total, d_attended.reshape(block_shape))
    )
    d_projected = jnp.concatenate(
        [
            d_queries.reshape(token_count, model_width),
            d_keys.reshape(token_count, model_width),
            d_values.reshape(token_count, model_width),
        ],
        axis=1,
    )
    d_normed = times_transpose(d_projected, weights_back[:, : 3 * model_width])
    unused, norm_pull_one = jax.vjp(normalize_layer, rows_in, params_back[:, 0], params_back[:, 1])
    d_rows_norm, d_gain_one, d_shift_one = norm_pull_one(d_normed)
    grad_tokens = (d_middle + d_rows_norm).astype(jnp.bfloat16)
    grad_w_local = jnp.concatenate(
        [
            contract_rows(normed, d_projected),
            contract_rows(attention_result, d_branch),
            contract_rows(normed_two, d_pre),
            contract_rows(cotangent, active),
        ],
        axis=1,
    )
    proj_sums = jnp.sum(d_projected.astype(jnp.float32), axis=0)
    small_cols = jnp.stack(
        [
            d_gain_one,
            d_shift_one,
            proj_sums[:model_width],
            proj_sums[2 * model_width :],
            jnp.sum(d_branch.astype(jnp.float32), axis=0),
            d_gain_two,
            d_shift_two,
            jnp.sum(back_rows, axis=0),
        ],
        axis=1,
    )
    grad_s_local = jnp.concatenate(
        [small_cols, jnp.sum(d_pre.astype(jnp.float32), axis=0).reshape(model_width, -1)], axis=1
    )
    part_w, part_s = (
        lax.psum_scatter(grad_w_local, "dp", scatter_dimension=1, tiled=True),
        lax.psum_scatter(grad_s_local, "dp", scatter_dimension=1, tiled=True),
    )
    part_w, part_s = (
        lax.psum_scatter(part_w, "fsdp", scatter_dimension=0, tiled=True),
        lax.psum_scatter(part_s, "fsdp", scatter_dimension=0, tiled=True),
    )
    grad_w, grad_s = (
        lax.all_gather(part_w, "dp", axis=1, tiled=True),
        lax.all_gather(part_s, "dp", axis=1, tiled=True),
    )
    row_count = grad_w.shape[0]
    block_width = model_width // 2
    block_count = grad_w.shape[1] // block_width
    owned_slots = first_moment.shape[0]
    devices = lax.axis_size("fsdp")
    slot_ids = jnp.arange(owned_slots * devices, dtype=jnp.int32)
    matches = block_slots[None, :] == slot_ids[:, None]
    in_use = jnp.any(matches, axis=1)
    source_block = jnp.sum(
        jnp.where(matches, jnp.arange(block_count, dtype=jnp.int32)[None, :], 0), axis=1
    )
    outgoing = jnp.take(grad_w.reshape(row_count, block_count, block_width), source_block, axis=1)
    outgoing = jnp.where(in_use[None, :, None], outgoing, 0.0).reshape(
        row_count, devices, owned_slots, block_width
    )
    incoming = lax.all_to_all(outgoing, "fsdp", split_axis=1, concat_axis=0, tiled=True).reshape(
        row_count * devices, owned_slots, block_width
    )
    my_use = lax.dynamic_slice_in_dim(in_use, lax.axis_index("fsdp") * owned_slots, owned_slots)
    eigen_turned = jnp.einsum("kdi,dkc->kic", left_bases, incoming, precision=EXACT_PRECISION)
    eigen_turned = jnp.einsum("kic,kcj->kij", eigen_turned, right_bases, precision=EXACT_PRECISION)
    first_new = BETA_FIRST * first_moment + (1.0 - BETA_FIRST) * eigen_turned
    second_new = BETA_SECOND * second_moment + (1.0 - BETA_SECOND) * eigen_turned * eigen_turned
    direction = adam_direction(first_new, second_new)
    rotated_gradient = jnp.einsum("kij,klj->kil", direction, right_bases, precision=EXACT_PRECISION)
    rotated_gradient = jnp.einsum(
        "kdi,kil->dkl", left_bases, rotated_gradient, precision=EXACT_PRECISION
    )
    returned = lax.all_to_all(
        rotated_gradient.reshape(devices, row_count, owned_slots, block_width),
        "fsdp",
        split_axis=0,
        concat_axis=0,
        tiled=True,
    )
    by_slot = jnp.moveaxis(returned, 1, 0).reshape(row_count, devices * owned_slots, block_width)
    update = jnp.take(by_slot, block_slots, axis=1).reshape(row_count, block_count * block_width)
    new_master = master - RATE_MATRIX * update
    new_copy = new_master.astype(jnp.bfloat16)
    keep_slot = my_use[:, None, None]
    new_first = jnp.where(keep_slot, first_new, 0.0)
    new_second = jnp.where(keep_slot, second_new, 0.0)
    new_small_first = BETA_FIRST * small_first + (1.0 - BETA_FIRST) * grad_s
    new_small_second = BETA_SECOND * small_second + (1.0 - BETA_SECOND) * grad_s * grad_s
    new_small = small_params - RATE_VECTOR * adam_direction(new_small_first, new_small_second)
    return (
        out_tokens,
        grad_tokens,
        grad_w,
        grad_s,
        new_first,
        new_second,
        new_master,
        new_copy,
        new_small,
        new_small_first,
        new_small_second,
        loss_accuracy,
        counts,
    )


def solution(mesh):
    return jax.shard_map(
        local,
        mesh=mesh,
        in_specs=(
            P(("dp", "fsdp"), None),
            P(("dp", "fsdp"), None),
            P(("dp", "fsdp")),
            P(("dp", "fsdp")),
            P(),
            P("fsdp", None),
            P("fsdp", None),
            P("fsdp", None),
            P("fsdp", None),
            P(),
            P("fsdp", None, None),
            P("fsdp", None, None),
            P("fsdp", None, None),
            P("fsdp", None, None),
        ),
        out_specs=(
            P(("dp", "fsdp"), None),
            P(("dp", "fsdp"), None),
            P("fsdp", None),
            P("fsdp", None),
            P("fsdp", None, None),
            P("fsdp", None, None),
            P("fsdp", None),
            P("fsdp", None),
            P("fsdp", None),
            P("fsdp", None),
            P("fsdp", None),
            P(),
            P(),
        ),
        check_vma=False,
    )
```

profile of v0, /device:TPU:0, one launch (start us, length us, event | category | flops | bytes accessed | tf_op | source)
XLA Modules:
  0.0 1169.3 jit_solution(2485766205392647652)
XLA Ops:
  7.3 3.8 convert_element_type.121
  11.2 33.4 %all-gather = bf16[8,80,16]{1,2,0:T(8,128)(2,1)S(1)} all-gather(bf16[1,80,16]{1,2,0:T(8,128)(2,1)S(1)} %convert_bitcast_fusion), channel_id=1, replica_groups=mesh['dp'=4,'fsdp'=8] {'fsdp'}, dimensions={0}, use_global_device_ids=true | all-gather | bytes 23040 | tf_op jit(solution)/shard_map/all_gather | solution.py:117
  46.0 190.6 %all-gather.5.cloned.1.call-done = bf16[640,12800]{1,0:T(8,128)(2,1)} async-done(((bf16[80,12800]{1,0:T(8,128)(2,1)}), bf16[640,12800]{1,0:T(8,128)(2,1)}) %all-gather.5.cloned.1.call-update) | async-done | bytes 16384016 | tf_op jit(solution)/shard_map/all_gather | solution.py:116
  236.6 2.8 fusion.29
  239.4 0.9 fusion.87
  240.5 1.3 copy.111
  241.8 2.0 copy.110
  243.8 0.9 multiply_reduce_fusion.1
  244.7 0.9 fusion.15
  245.7 1.1 fusion.45
  247.3 1.9 slice-done.3
  249.2 1.4 slice-done.4
  250.6 1.1 slice-done.5
  252.5 15.0 %multiply_convert_fusion.1 = (bf16[256,5120]{1,0:T(8,128)(2,1)}, f32[256,5120]{1,0:T(8,128)}, f32[256,5120]{1,0:T(8,128)}) fusion(f32[5120]{0:T(1024)S(1)} %add.172, bf16[640,12800]{1,0:T(8,128)(2,1)S(1)} %bitcast.115, f32[256,640]{1,0:T(8,128)S(1)} %get-tuple-element.106, f32[640]{0:T(1024)S(1)} %get-tuple-element.67, f32[640]{0:T(1024)S(1)} %get-tuple-element.68, ...), kind=kOutput, calls=%fused_computation.21 | convolution fusion | flops 1765048320 | bytes 20346880 | tf_op jit(solution)/shard_map/dot_general | solution.py:150
  267.5 6.6 convert_reduce_fusion
  274.1 2.4 multiply_reduce_fusion.2
  276.9 0.9 copy-done.6
  278.0 1.6 fusion.92
  279.5 1.2 convolution_convert_fusion
  280.7 1.9 copy.115
  282.6 3.7 fusion.48
  286.9 1.4 multiply_reduce_fusion
  288.3 1.4 multiply_convert_fusion
  291.4 6.7 fusion.80
  298.1 6.6 convolution_bitcast_fusion
  304.7 3.3 fusion.76
  308.0 21.8 %pad_maximum_fusion = f32[640,12800]{1,0:T(8,128)} fusion(f32[640,5120]{1,0:T(8,128)} %convolution_bitcast_fusion, f32[640,5120]{1,0:T(8,128)} %fusion.80, f32[640,640]{1,0:T(8,128)S(1)} %copy-done.5, f32[640,1920]{1,0:T(8,128)} %fusion.76), kind=kLoop, calls=%fused_computation.2 | loop fusion | flops 24576000 | bytes 65536000 | tf_op jit(solution)/shard_map/concatenate | solution.py:218
  329.9 225.7 %reduce-scatter.5.cloned.1.call-done = f32[640,3200]{1,0:T(8,128)} async-done(((f32[640,12800]{1,0:T(8,128)}), f32[640,3200]{1,0:T(8,128)}) %reduce-scatter.5.cloned.1.call-update) | async-done | bytes 8192016 | tf_op jit(solution)/shard_map/reduce_scatter | solution.py:245
  555.7 149.0 %reduce-scatter.7.cloned.1.call-done = f32[80,3200]{1,0:T(8,128)} async-done(((f32[640,3200]{1,0:T(8,128)}), f32[80,3200]{1,0:T(8,128)}) %reduce-scatter.7.cloned.1.call-update) | async-done | bytes 1024016 | tf_op jit(solution)/shard_map/reduce_scatter | solution.py:249
  705.0 34.2 %all-gather.7.cloned.1.call-done = f32[80,12800]{1,0:T(8,128)} async-done(((f32[80,3200]{1,0:T(8,128)}), f32[80,12800]{1,0:T(8,128)}) %all-gather.7.cloned.1.call-update) | async-done | bytes 4096016 | tf_op jit(solution)/shard_map/all_gather | solution.py:253
  739.2 5.7 reshape.267
  744.9 5.5 copy.130
  750.4 5.5 gather_fusion
  755.9 5.6 bitcast_select_fusion
  761.6 5.5 all-to-all-start
  767.1 109.1 %all-to-all-done = f32[80,8,5,320]{3,0,2,1:T(8,128)} async-done(((f32[80,8,5,320]{3,0,2,1:T(8,128)}), f32[80,8,5,320]{3,0,2,1:T(8,128)}, u32[]{:S(2)}, u32[]{:S(2)}) %all-to-all-start) | async-done | bytes 4096032 | tf_op jit(solution)/shard_map/all_to_all | solution.py:271
  876.2 2.8 copy.131
  879.0 33.4 %fusion.93 = f32[5,320,640]{2,1,0:T(8,128)S(1)} fusion(f32[640,5,320]{2,0,1:T(8,128)S(1)} %bitcast.89, f32[5,640,640]{2,1,0:T(8,128)} %param.28), kind=kOutput, calls=%fused_computation.168 | convolution fusion | flops 7864320000 | bytes 16384000 | tf_op jit(solution)/shard_map/kdi,dkc->kic/dot_general | solution.py:275
  912.4 18.5 %broadcast_select_fusion = (f32[5,640,320]{1,2,0:T(8,128)}, f32[5,640,320]{1,2,0:T(8,128)}, f32[5,640,320]{1,2,0:T(8,128)}) fusion(pred[5]{0:T(512)(128)(4,1)S(1)} %dynamic_slice.21, f32[5,640,320]{1,2,0:T(8,128)} %param.27, f32[5,640,320]{1,2,0:T(8,128)} %param.26, f32[5,320,640]{2,1,0:T(8,128)S(1)} %fusion.93, f32[5,320,320]{2,1,0:T(8,128)S(1)} %copy-done), kind=kOutput, calls=%fused_computation.61 | convolution fusion | flops 3940352000 | bytes 26624004 | tf_op jit(solution)/shard_map/kic,kcj->kij/dot_general | solution.py:276
  930.9 19.0 %fusion.17 = f32[5,640,320]{1,2,0:T(8,128)S(1)} fusion(f32[5,320,320]{2,1,0:T(8,128)S(1)} %copy-done, f32[5,640,320]{1,2,0:T(8,128)} %get-tuple-element.114, f32[5,640,320]{1,2,0:T(8,128)} %param.26, f32[5,640,320]{1,2,0:T(8,128)} %param.27), kind=kOutput, calls=%fused_computation.42 | convolution fusion | flops 3942400000 | bytes 18432000 | tf_op jit(solution)/shard_map/kij,klj->kil/dot_general | solution.py:280
  950.0 20.1 %convolution_bitcast_fusion.1 = f32[640,5,320]{0,2,1:T(8,128)} fusion(f32[5,640,320]{1,2,0:T(8,128)S(1)} %fusion.17, f32[5,640,640]{2,1,0:T(8,128)S(1)} %bitcast.87), kind=kOutput, calls=%fused_computation.58 | convolution fusion | flops 7864320000 | bytes 16384000 | tf_op jit(solution)/shard_map/kdi,kil->dkl/dot_general | solution.py:281
  970.2 6.6 copy.134
  976.7 4.9 copy.135
  981.7 4.7 all-to-all-start.1
  988.0 0.9 reshape.266
  989.8 0.9 stack.38
  991.6 1.6 convert_reduce_fusion.1
  994.0 3.1 fusion.81
  997.6 1.1 convert_reduce_fusion.3
  998.8 0.9 stack.39
  1002.3 2.3 concatenate.21
  1004.6 15.0 %all-reduce = f32[640,16]{1,0:T(8,128)} all-reduce(f32[640,16]{1,0:T(8,128)S(1)} %concatenate.21), channel_id=4, replica_groups=mesh['dp'=4,'fsdp'=8] {'dp'}, use_global_device_ids=true, to_apply=%region_21.22.clone | all-reduce | flops 10240 | bytes 81920
  1019.6 1.8 constant_dynamic-slice_fusion
  1021.5 5.9 fusion.42
  1029.3 88.3 %all-reduce.1 = (f32[4]{0:T(128)S(1)}, f32[5]{0:T(128)S(1)}) all-reduce(f32[4]{0:T(128)S(1)} %get-tuple-element.77, f32[5]{0:T(128)S(1)} %pad_maximum_fusion.3), channel_id=1, replica_groups=mesh['dp'=4,'fsdp'=8] {'dp','fsdp'}, use_global_device_ids=true, to_apply=%region_33.35 | all-reduce | flops 9 | bytes 72 | tf_op jit(solution)/shard_map/psum | solution.py:174
  1117.6 1.1 fusion.89
  1120.0 8.9 reduce-scatter.9.cloned.1.call-done
  1129.7 5.2 all-gather.1
  1135.5 5.5 gather_fusion.1
  1141.0 3.0 bitcast_multiply_fusion
  1144.1 3.7 copy.136
  1147.8 5.5 mul.298
  1153.3 6.7 fusion.83
  1160.0 2.0 copy.148
  (153 shorter events, 17.4 us)
Async XLA Ops:
  7.2 905.2 %copy-start = (f32[5,320,320]{2,1,0:T(8,128)S(1)}, f32[5,320,320]{2,1,0:T(8,128)}, u32[]{:S(2)}) copy-start(f32[5,320,320]{2,1,0:T(8,128)} %param.29) | copy-start | bytes 6144004
  7.2 4.0 copy-start.25
  7.2 38.5 %copy-start.4 = (bf16[256,640]{1,0:T(8,128)(2,1)S(1)}, bf16[256,640]{1,0:T(8,128)(2,1)}, u32[]{:S(2)}) copy-start(bf16[256,640]{1,0:T(8,128)(2,1)} %param.16) | copy-start | bytes 983044
  7.2 229.4 %all-gather.5.cloned.1.call-start = ((), (), s32[]{:S(2)}) async-start(), calls=%async_computation.5 | async-start | bytes 18432000 | tf_op jit(solution)/shard_map/all_gather | solution.py:116
  11.1 544.6 %reduce-scatter.5.cloned.1.call-start = ((), (), s32[]{:S(2)}) async-start(), calls=%async_computation.6 | async-start | bytes 40960000 | tf_op jit(solution)/shard_map/reduce_scatter | solution.py:245
  46.0 198.6 %copy-start.27 = (f32[256]{0:T(256)}, f32[256]{0:T(256)S(1)}, u32[]{:S(2)}) copy-start(f32[256]{0:T(256)S(1)} %fusion.63) | copy-start | bytes 3076
  240.5 5.1 copy-start.12
  241.7 3.9 copy-start.14
  243.8 1.9 copy-start.22
  243.8 3.6 slice-start.2
  244.7 2.7 copy-start.1
  244.7 4.5 slice-start.3
  245.6 4.9 slice-start.4
  245.7 6.0 slice-start.5
  252.5 15.0 %copy-start.16 = (bf16[256,640]{1,0:T(8,128)(2,1)S(1)}, bf16[256,640]{1,0:T(8,128)(2,1)}, u32[]{:S(2)}) copy-start(bf16[256,640]{1,0:T(8,128)(2,1)} %param.17) | copy-start | bytes 983044
  274.1 2.4 copy-start.19
  276.9 0.9 copy-start.6
  282.6 4.1 copy-start.2
  282.6 4.2 copy-start.9
  282.6 4.3 copy-start.23
  286.9 17.8 %copy-start.8 = (bf16[20,32,256]{2,1,0:T(8,128)(2,1)}, bf16[20,32,256]{2,1,0:T(8,128)(2,1)S(1)}, u32[]{:S(2)}) copy-start(bf16[20,32,256]{2,1,0:T(8,128)(2,1)S(1)} %fusion.48) | copy-start | bytes 983044
  288.2 1.4 copy-start.15
  288.2 2.3 copy-start.13
  289.7 1.7 copy-start.20
  290.6 14.1 %copy-start.10 = (bf16[20,32,256]{2,1,0:T(8,128)(2,1)}, bf16[20,32,256]{2,1,0:T(8,128)(2,1)S(1)}, u32[]{:S(2)}) copy-start(bf16[20,32,256]{2,1,0:T(8,128)(2,1)S(1)} %fusion.47) | copy-start | bytes 983044
  291.4 13.3 %copy-start.11 = (bf16[20,32,256]{2,1,0:T(8,128)(2,1)}, bf16[20,32,256]{2,1,0:T(8,128)(2,1)S(1)}, u32[]{:S(2)}) copy-start(bf16[20,32,256]{2,1,0:T(8,128)(2,1)S(1)} %fusion.46) | copy-start | bytes 983044
  291.4 6.7 copy-start.17
  291.4 6.7 copy-start.21
  304.7 3.3 copy-start.5
  329.9 374.9 %copy-start.35 = (s32[40]{0:T(128)S(1)}, s32[40]{0:T(128)}, u32[]{:S(2)}) copy-start(s32[40]{0:T(128)} %param.25) | copy-start | bytes 484
  329.9 374.8 %reduce-scatter.7.cloned.1.call-start = ((), (), s32[]{:S(2)}) async-start(), calls=%async_computation.7 | async-start | bytes 9216000 | tf_op jit(solution)/shard_map/reduce_scatter | solution.py:249
  555.7 183.5 %all-gather.7.cloned.1.call-start = ((), (), s32[]{:S(2)}) async-start(), calls=%async_computation.8 | async-start | bytes 5120000 | tf_op jit(solution)/shard_map/all_gather | solution.py:253
  761.6 114.7 %all-to-all-start = ((f32[80,8,5,320]{3,0,2,1:T(8,128)}), f32[80,8,5,320]{3,0,2,1:T(8,128)}, u32[]{:S(2)}, u32[]{:S(2)}) async-start(f32[80,8,5,320]{3,0,2,1:T(8,128)} %bitcast.88), calls=%async_computation.3 | async-start | bytes 9830400 | tf_op jit(solution)/shard_map/all_to_all | solution.py:271
  879.0 71.0 %slice-start = ((s8[8192000]{0:T(1024)(128)(4,1)}), s8[4194304]{0:T(1024)(128)(4,1)S(1)}, s32[]{:S(2)}) async-start(s8[8192000]{0:T(1024)(128)(4,1)} %bitcast.86), calls=%async_computation.10 | async-start | bytes 8388608
  912.4 37.6 %slice-start.1 = ((s8[8192000]{0:T(1024)(128)(4,1)}), s8[3997696]{0:T(1024)(128)(4,1)S(1)}, s32[]{:S(2)}) async-start(s8[8192000]{0:T(1024)(128)(4,1)} %bitcast.86), calls=%async_computation.11 | async-start | bytes 7995392
  981.7 5.0 copy-start.32
  981.7 5.0 copy-start.36
  981.7 153.8 %all-to-all-start.1 = ((f32[8,80,5,320]{3,1,2,0:T(8,128)}), f32[8,80,5,320]{3,1,2,0:T(8,128)}, u32[]{:S(2)}, u32[]{:S(2)}) async-start(f32[8,80,5,320]{3,1,2,0:T(8,128)} %copy.135), calls=%async_computation.4 | async-start | bytes 9830400 | tf_op jit(solution)/shard_map/all_to_all | solution.py:284
  986.4 142.4 %reduce-scatter.9.cloned.1.call-start = ((), (), s32[]{:S(2)}) async-start(), calls=%async_computation.9 | async-start | bytes 368640 | tf_op jit(solution)/shard_map/reduce_scatter | solution.py:250
  988.9 8.3 copy-start.28
  991.6 6.1 copy-start.7
  991.6 6.1 copy-start.18
  997.2 24.3 %copy-start.34 = (f32[640]{0:T(1024)S(1)}, f32[640]{0:T(1024)}, u32[]{:S(2)}) copy-start(f32[640]{0:T(1024)} %get-tuple-element.66) | copy-start | bytes 7684
  1021.5 6.0 copy-start.31
  1021.5 6.3 copy-start.33
  1021.5 113.4 %copy-start.26 = (f32[80,16]{0,1:T(8,128)S(1)}, f32[80,16]{0,1:T(8,128)}, u32[]{:S(2)}) copy-start(f32[80,16]{0,1:T(8,128)} %param.22) | copy-start | bytes 15364
  1021.5 113.4 %copy-start.29 = (f32[80,16]{0,1:T(8,128)S(1)}, f32[80,16]{0,1:T(8,128)}, u32[]{:S(2)}) copy-start(f32[80,16]{0,1:T(8,128)} %param.23) | copy-start | bytes 15364
  1021.5 113.4 %copy-start.30 = (f32[80,16]{0,1:T(8,128)S(1)}, f32[80,16]{0,1:T(8,128)}, u32[]{:S(2)}) copy-start(f32[80,16]{0,1:T(8,128)} %param.24) | copy-start | bytes 15364
  1027.5 116.6 %copy-start.24 = (bf16[256,640]{1,0:T(8,128)(2,1)}, bf16[256,640]{1,0:T(8,128)(2,1)S(1)}, u32[]{:S(2)}) copy-start(bf16[256,640]{1,0:T(8,128)(2,1)S(1)} %fusion.42) | copy-start | bytes 983044
  1153.3 6.7 copy-start.3
Sparse Core Ops, SparseCore 0:
  11.2 225.3 all-gather.4
  330.0 225.6 reduce-scatter.4
  559.4 145.2 reduce-scatter.6
  706.1 32.9 all-gather.6
  1021.6 107.2 reduce-scatter.8
where the time goes:
time: 1180 us; the launch traced here: 1170 us
  waiting for transfers between devices  717 us (61%)
  matrix products  156 us (13%)
  blocking collectives  142 us (12%)
  local copies, waits for them, and re-layouts  76.1 us (6%)
  other arithmetic  51.6 us (4%)
  between operations  16 us (1%)
    reduce_scatter x1, waiting for transfers between devices, local(): lax.psum_scatter(grad_w_local, 'dp', scatter_dimension=1, tiled=True)  226 us
    all_gather x1, waiting for transfers between devices, local(): lax.all_gather(local_weights, 'fsdp', axis=0, tiled=True)  191 us
    reduce_scatter x1, waiting for transfers between devices, local(): lax.psum_scatter(part_w, 'fsdp', scatter_dimension=0, tiled=True)  149 us
    all_to_all x1, waiting for transfers between devices, local(): lax.all_to_all(outgoing, 'fsdp', split_axis=1, concat_axis=0, tiled=True)  109 us
    psum x1, blocking collectives, local(): lax.psum((local_sums, jnp.sum(chosen, axis=0)), ('dp', 'fsdp'))  88.3 us
    all_gather x1, waiting for transfers between devices, local(): lax.all_gather(part_w, 'dp', axis=1, tiled=True)  34.2 us
    all_gather x1, blocking collectives, local(): lax.all_gather(local_small, 'fsdp', axis=0, tiled=True)  33.4 us
    dot_general x1, matrix products, local(): jnp.einsum('kdi,dkc->kic', left_bases, incoming, precision=EXACT_PRECISION)  33.4 us
  transfers between devices with their start and end apart: 7, of which 6 were waited for; matrix products, arithmetic and copies ran while one was open for 3% of the time, Pallas kernels for 0%

commit v1 on v0

--- a/solution.py
+++ b/solution.py
@@ -13,6 +13,19 @@
 RATE_MATRIX = 0.02
 RATE_VECTOR = 0.05
 EXACT_PRECISION = lax.Precision.HIGHEST
+
+
+def ring_gather(shard, axis, dim):
+    ways = lax.axis_size(axis)
+    up = [(d, (d + 1) % ways) for d in range(ways)]
+    down = [(d, (d - 1) % ways) for d in range(ways)]
+    earlier, later = ([shard], [shard])
+    for _ in range(ways // 2):
+        earlier.append(lax.ppermute(earlier[-1], axis, up))
+    for _ in range((ways - 1) // 2):
+        later.append(lax.ppermute(later[-1], axis, down))
+    line = jnp.concatenate([*earlier[::-1], *later[1:]], axis=dim)
+    return jnp.roll(line, (lax.axis_index(axis) - ways // 2) * shard.shape[dim], axis=dim)
 
 
 def normalize_layer(rows_in, norm_gain, norm_shift):
@@ -113,7 +126,7 @@
     local_weights = master.astype(jnp.bfloat16)
     local_small = small_params.astype(jnp.bfloat16)
     weights, small_all = (
-        lax.all_gather(local_weights, "fsdp", axis=0, tiled=True),
+        ring_gather(local_weights, "fsdp", 0),
         lax.all_gather(local_small, "fsdp", axis=0, tiled=True),
     )
     params = small_all.astype(jnp.float32)

time: 1180 us -> 1540 us (1.31)
  waiting for transfers between devices: 717 us -> 889 us
  blocking collectives: 142 us -> 267 us
  local copies, waits for them, and re-layouts: 76.1 us -> 106 us
  starting transfers between devices: 10.6 us -> 26.3 us
    ppermute x0 -> x7, waiting for transfers between devices: none -> 280 us  [the longest x4 215 us: ring_gather(): earlier.append(lax.ppermute(earlier[-1], axis, up))]
    all_gather x1, waiting for transfers between devices: 191 us -> 19.3 us  [local(): lax.all_gather(local_weights, 'fsdp', axis=0, tiled=True)]
    all_gather x1, blocking collectives: 33.4 us -> 130 us  [local(): lax.all_gather(local_small, 'fsdp', axis=0, tiled=True)]
    reduce_scatter x1, waiting for transfers between devices: 8.85 us -> 61.2 us  [local(): lax.psum_scatter(part_s, 'fsdp', scatter_dimension=0, tiled=True)]
    unnamed x91 -> x120, local copies, waits for them, and re-layouts: 12.7 us -> 43.6 us
    psum x1, blocking collectives: 88.3 us -> 117 us  [local(): lax.psum((local_sums, jnp.sum(chosen, axis=0)), ('dp', 'fsdp'))]
  transfers between devices with their start and end apart: 7 -> 14, of which waited for: 6 -> 10; matrix products, arithmetic and copies ran while one was open for 3% -> 7% of each run, Pallas kernels for 0% -> 0%
where the time goes in v1:
time: 1540 us; the launch traced here: 1530 us
  waiting for transfers between devices  889 us (58%)
  blocking collectives  267 us (17%)
  matrix products  171 us (11%)
  local copies, waits for them, and re-layouts  106 us (7%)
  other arithmetic  53.3 us (3%)
  starting transfers between devices  26.3 us (2%)
  between operations  16.5 us (1%)
    reduce_scatter x1, waiting for transfers between devices, local(): lax.psum_scatter(grad_w_local, 'dp', scatter_dimension=1, tiled=True)  236 us
    ppermute x4, waiting for transfers between devices, ring_gather(): earlier.append(lax.ppermute(earlier[-1], axis, up))  215 us
    reduce_scatter x1, waiting for transfers between devices, local(): lax.psum_scatter(part_w, 'fsdp', scatter_dimension=0, tiled=True)  149 us
    all_gather x1, blocking collectives, local(): lax.all_gather(local_small, 'fsdp', axis=0, tiled=True)  130 us
    psum x1, blocking collectives, local(): lax.psum((local_sums, jnp.sum(chosen, axis=0)), ('dp', 'fsdp'))  117 us
    all_to_all x1, waiting for transfers between devices, local(): lax.all_to_all(outgoing, 'fsdp', split_axis=1, concat_axis=0, tiled=True)  109 us
    ppermute x3, waiting for transfers between devices, ring_gather(): later.append(lax.ppermute(later[-1], axis, down))  65.4 us
    reduce_scatter x1, waiting for transfers between devices, local(): lax.psum_scatter(part_s, 'fsdp', scatter_dimension=0, tiled=True)  61.2 us
  transfers between devices with their start and end apart: 14, of which 10 were waited for; matrix products, arithmetic and copies ran while one was open for 7% of the time, Pallas kernels for 0%

profile of v1, /device:TPU:0, one launch (start us, length us, event | category | flops | bytes accessed | tf_op | source)
XLA Modules:
  0.0 1528.3 jit_solution(1051537121998559756)
XLA Ops:
  7.3 3.8 convert_element_type.121
  11.1 3.0 collective-permute-start
  14.1 47.8 %collective-permute-done = bf16[80,12800]{1,0:T(8,128)(2,1)S(1)} collective-permute-done((bf16[80,12800]{1,0:T(8,128)(2,1)}, bf16[80,12800]{1,0:T(8,128)(2,1)S(1)}, u32[]{:S(2)}, u32[]{:S(2)}) %collective-permute-start) | collective-permute-done | bytes 2048032 | tf_op jit(solution)/shard_map/ppermute | solution.py:24
  63.2 4.7 collective-permute-start.4
  67.9 82.7 %collective-permute-done.1 = bf16[80,12800]{1,0:T(8,128)(2,1)S(1)} collective-permute-done((bf16[80,12800]{1,0:T(8,128)(2,1)S(1)}, bf16[80,12800]{1,0:T(8,128)(2,1)S(1)}, u32[]{:S(2)}, u32[]{:S(2)}) %collective-permute-start.1) | collective-permute-done | bytes 2048032 | tf_op jit(solution)/shard_map/ppermute | solution.py:24
  151.9 2.5 collective-permute-start.2
  154.4 2.2 collective-permute-start.5
  156.6 84.3 %collective-permute-done.2 = bf16[80,12800]{1,0:T(8,128)(2,1)} collective-permute-done((bf16[80,12800]{1,0:T(8,128)(2,1)S(1)}, bf16[80,12800]{1,0:T(8,128)(2,1)}, u32[]{:S(2)}, u32[]{:S(2)}) %collective-permute-start.2) | collective-permute-done | bytes 2048032 | tf_op jit(solution)/shard_map/ppermute | solution.py:24
  241.0 2.6 collective-permute-start.3
  243.7 129.9 %all-gather = bf16[8,80,16]{1,2,0:T(8,128)(2,1)S(1)} all-gather(bf16[1,80,16]{1,2,0:T(8,128)(2,1)S(1)} %convert_bitcast_fusion), channel_id=1, replica_groups=mesh['dp'=4,'fsdp'=8] {'fsdp'}, dimensions={0}, use_global_device_ids=true | all-gather | bytes 23040 | tf_op jit(solution)/shard_map/all_gather | solution.py:130
  375.2 3.2 constant_dynamic-update-slice_fusion.15
  378.4 3.2 constant_dynamic-update-slice_fusion.14
  386.0 3.0 constant_dynamic-update-slice_fusion.10
  389.0 3.1 constant_dynamic-update-slice_fusion.9
  392.1 65.4 %collective-permute-done.6 = bf16[80,12800]{1,0:T(8,128)(2,1)S(1)} collective-permute-done((bf16[80,12800]{1,0:T(8,128)(2,1)}, bf16[80,12800]{1,0:T(8,128)(2,1)S(1)}, u32[]{:S(2)}, u32[]{:S(2)}) %collective-permute-start.6) | collective-permute-done | bytes 2048032 | tf_op jit(solution)/shard_map/ppermute | solution.py:26
  458.9 3.0 constant_dynamic-update-slice_fusion.7
  461.9 3.0 constant_dynamic-update-slice_fusion.6
  467.8 1.6 constant_dynamic-update-slice_fusion.3
  469.4 3.1 constant_dynamic-update-slice_fusion.2
  472.5 3.0 constant_dynamic-update-slice_fusion.1
  477.0 2.8 fusion.33
  486.2 2.1 fusion.95
  488.5 18.4 %multiply_convert_fusion.1 = (bf16[256,5120]{1,0:T(8,128)(2,1)S(1)}, f32[256,5120]{1,0:T(8,128)}, f32[256,5120]{1,0:T(8,128)}) fusion(f32[5120]{0:T(1024)S(1)} %add.185, bf16[1280,12800]{1,0:T(8,128)(2,1)} %constant_dynamic-update-slice_fusion, s32[]{:T(128)S(6)} %select_n.49, s32[]{:T(128)S(6)} %add.222, f32[256,640]{1,0:T(8,128)S(1)} %get-tuple-element.106, ...), kind=kOutput, calls=%fused_computation.22 | convolution fusion | flops 1765048320 | bytes 20343816 | tf_op jit(solution)/shard_map/dot_general | solution.py:163
  508.4 6.7 convolution_bitcast_fusion
  515.1 19.3 %all-gather.5.cloned.1.call-done = bf16[640,12800]{1,0:T(8,128)(2,1)} async-done(((bf16[80,12800]{1,0:T(8,128)(2,1)}), bf16[640,12800]{1,0:T(8,128)(2,1)}) %all-gather.5.cloned.1.call-update) | async-done | bytes 16384016 | tf_op jit(solution)/shard_map/all_gather | solution.py:196
  534.4 9.6 convert_reduce_fusion
  544.1 6.2 multiply_reduce_fusion.2
  552.3 2.3 convolution_convert_fusion
  554.7 1.9 copy.115
  556.5 3.7 fusion.52
  560.3 4.0 multiply_reduce_fusion
  567.6 6.7 fusion.85
  574.7 3.2 fusion.81
  578.0 21.6 %pad_maximum_fusion = f32[640,12800]{1,0:T(8,128)} fusion(f32[640,5120]{1,0:T(8,128)} %convolution_bitcast_fusion, f32[640,5120]{1,0:T(8,128)} %fusion.85, f32[640,640]{1,0:T(8,128)S(1)} %fusion.97, f32[640,1920]{1,0:T(8,128)} %fusion.81), kind=kLoop, calls=%fused_computation.2 | loop fusion | flops 24576000 | bytes 65536000 | tf_op jit(solution)/shard_map/concatenate | solution.py:231
  599.7 235.6 %reduce-scatter.5.cloned.1.call-done = f32[640,3200]{1,0:T(8,128)} async-done(((f32[640,12800]{1,0:T(8,128)}), f32[640,3200]{1,0:T(8,128)}) %reduce-scatter.5.cloned.1.call-update) | async-done | bytes 8192016 | tf_op jit(solution)/shard_map/reduce_scatter | solution.py:258
  835.4 148.9 %reduce-scatter.7.cloned.1.call-done = f32[80,3200]{1,0:T(8,128)} async-done(((f32[640,3200]{1,0:T(8,128)}), f32[80,3200]{1,0:T(8,128)}) %reduce-scatter.7.cloned.1.call-update) | async-done | bytes 1024016 | tf_op jit(solution)/shard_map/reduce_scatter | solution.py:262
  984.6 34.2 %all-gather.7.cloned.1.call-done = f32[80,12800]{1,0:T(8,128)} async-done(((f32[80,3200]{1,0:T(8,128)}), f32[80,12800]{1,0:T(8,128)}) %all-gather.7.cloned.1.call-update) | async-done | bytes 4096016 | tf_op jit(solution)/shard_map/all_gather | solution.py:266
  1018.8 5.7 reshape.267
  1024.5 5.5 copy.130
  1030.0 5.5 gather_fusion
  1035.5 5.6 bitcast_select_fusion
  1041.2 6.0 all-to-all-start
  1047.2 109.0 %all-to-all-done = f32[80,8,5,320]{3,0,2,1:T(8,128)} async-done(((f32[80,8,5,320]{3,0,2,1:T(8,128)}), f32[80,8,5,320]{3,0,2,1:T(8,128)}, u32[]{:S(2)}, u32[]{:S(2)}) %all-to-all-start) | async-done | bytes 4096032 | tf_op jit(solution)/shard_map/all_to_all | solution.py:284
  1156.2 2.8 copy.131
  1159.0 33.4 %fusion.98 = f32[5,320,640]{2,1,0:T(8,128)S(1)} fusion(f32[640,5,320]{2,0,1:T(8,128)S(1)} %bitcast.91, f32[5,640,640]{2,1,0:T(8,128)} %param.28), kind=kOutput, calls=%fused_computation.186 | convolution fusion | flops 7864320000 | bytes 16384000 | tf_op jit(solution)/shard_map/kdi,dkc->kic/dot_general | solution.py:288
  1192.4 18.5 %broadcast_select_fusion = (f32[5,640,320]{1,2,0:T(8,128)}, f32[5,640,320]{1,2,0:T(8,128)}, f32[5,640,320]{1,2,0:T(8,128)}) fusion(pred[5]{0:T(512)(128)(4,1)S(1)} %dynamic_slice.26, f32[5,640,320]{1,2,0:T(8,128)} %param.27, f32[5,640,320]{1,2,0:T(8,128)} %param.26, f32[5,320,640]{2,1,0:T(8,128)S(1)} %fusion.98, f32[5,320,320]{2,1,0:T(8,128)S(1)} %copy-done), kind=kOutput, calls=%fused_computation.62 | convolution fusion | flops 3940352000 | bytes 26624004 | tf_op jit(solution)/shard_map/kic,kcj->kij/dot_general | solution.py:289
  1210.9 19.0 %fusion.21 = f32[5,640,320]{1,2,0:T(8,128)S(1)} fusion(f32[5,320,320]{2,1,0:T(8,128)S(1)} %copy-done, f32[5,640,320]{1,2,0:T(8,128)} %get-tuple-element.114, f32[5,640,320]{1,2,0:T(8,128)} %param.26, f32[5,640,320]{1,2,0:T(8,128)} %param.27), kind=kOutput, calls=%fused_computation.43 | convolution fusion | flops 3942400000 | bytes 18432000 | tf_op jit(solution)/shard_map/kij,klj->kil/dot_general | solution.py:293
  1230.0 20.0 %convolution_bitcast_fusion.1 = f32[640,5,320]{0,2,1:T(8,128)} fusion(f32[5,640,320]{1,2,0:T(8,128)S(1)} %fusion.21, f32[5,640,640]{2,1,0:T(8,128)S(1)} %bitcast.89), kind=kOutput, calls=%fused_computation.59 | convolution fusion | flops 7864320000 | bytes 16384000 | tf_op jit(solution)/shard_map/kdi,kil->dkl/dot_general | solution.py:294
  1249.9 6.6 copy.134
  1256.5 4.9 copy.135
  1261.4 4.7 all-to-all-start.1
  1267.9 7.3 fusion.47
  1277.7 116.8 %all-reduce.1 = (f32[4]{0:T(128)S(1)}, f32[5]{0:T(128)S(1)}) all-reduce(f32[4]{0:T(128)S(1)} %get-tuple-element.77, f32[5]{0:T(128)S(1)} %pad_maximum_fusion.3), channel_id=1, replica_groups=mesh['dp'=4,'fsdp'=8] {'dp','fsdp'}, use_global_device_ids=true, to_apply=%region_33.35 | all-reduce | flops 9 | bytes 72 | tf_op jit(solution)/shard_map/psum | solution.py:187
  1396.3 3.2 fusion.86
  1408.0 2.2 concatenate.28
  1410.2 14.4 all-reduce
  1426.1 61.2 %reduce-scatter.9.cloned.1.call-done = f32[80,4]{1,0:T(8,128)} async-done(((f32[640,4]{1,0:T(8,128)}), f32[80,4]{1,0:T(8,128)}) %reduce-scatter.9.cloned.1.call-update) | async-done | bytes 1296 | tf_op jit(solution)/shard_map/reduce_scatter | solution.py:263
  1488.1 5.5 all-gather.1
  1494.3 5.5 gather_fusion.1
  1499.8 3.0 bitcast_multiply_fusion
  1502.8 3.7 copy.136
  1506.5 5.5 mul.302
  1512.0 6.7 fusion.88
  1518.7 2.0 copy.163
  (199 shorter events, 45.1 us)
Async XLA Ops:
  7.2 1185.2 %copy-start = (f32[5,320,320]{2,1,0:T(8,128)S(1)}, f32[5,320,320]{2,1,0:T(8,128)}, u32[]{:S(2)}) copy-start(f32[5,320,320]{2,1,0:T(8,128)} %param.29) | copy-start | bytes 6144004
  7.2 236.5 %copy-start.35 = (f32[80,16]{0,1:T(8,128)S(1)}, f32[80,16]{0,1:T(8,128)}, u32[]{:S(2)}) copy-start(f32[80,16]{0,1:T(8,128)} %param.22) | copy-start | bytes 15364
  7.2 367.5 %copy-start.4 = (bf16[256,640]{1,0:T(8,128)(2,1)S(1)}, bf16[256,640]{1,0:T(8,128)(2,1)}, u32[]{:S(2)}) copy-start(bf16[256,640]{1,0:T(8,128)(2,1)} %param.16) | copy-start | bytes 983044
  7.2 527.2 %all-gather.5.cloned.1.call-start = ((), (), s32[]{:S(2)}) async-start(), calls=%async_computation.5 | async-start | bytes 18432000 | tf_op jit(solution)/shard_map/all_gather | solution.py:196
  11.1 50.8 %collective-permute-start = (bf16[80,12800]{1,0:T(8,128)(2,1)}, bf16[80,12800]{1,0:T(8,128)(2,1)S(1)}, u32[]{:S(2)}, u32[]{:S(2)}) collective-permute-start(bf16[80,12800]{1,0:T(8,128)(2,1)} %convert_element_type.121), channel_id=1, source_target_pairs={{0,1},{1,2},{2,3},{3,4},{4,5},{5,6},{6,7},{7,0},{8,9},{9,10},{10,1... | collective-permute-start | bytes 6144008 | tf_op jit(solution)/shard_map/ppermute | solution.py:24
  61.9 1.3 copy-start.5
  63.2 87.4 %collective-permute-start.1 = (bf16[80,12800]{1,0:T(8,128)(2,1)S(1)}, bf16[80,12800]{1,0:T(8,128)(2,1)S(1)}, u32[]{:S(2)}, u32[]{:S(2)}) collective-permute-start(bf16[80,12800]{1,0:T(8,128)(2,1)S(1)} %collective-permute-done), channel_id=1, source_target_pairs={{0,1},{1,2},{2,3},{3,4},{4,5},{5,6},{6,7},{7,0},{8,9},{9,10},{10,1... | collective-permute-start | bytes 6144008 | tf_op jit(solution)/shard_map/ppermute | solution.py:24
  63.2 91.2 %collective-permute-start.4 = (bf16[80,12800]{1,0:T(8,128)(2,1)}, bf16[80,12800]{1,0:T(8,128)(2,1)}, u32[]{:S(2)}, u32[]{:S(2)}) collective-permute-start(bf16[80,12800]{1,0:T(8,128)(2,1)} %convert_element_type.121), channel_id=1, source_target_pairs={{0,7},{1,0},{2,1},{3,2},{4,3},{5,4},{6,5},{7,6},{8,15},{9,8},{10,9... | collective-permute-start | bytes 6144008 | tf_op jit(solution)/shard_map/ppermute | solution.py:26
  150.6 1.3 copy-start.7
  151.9 89.1 %collective-permute-start.2 = (bf16[80,12800]{1,0:T(8,128)(2,1)S(1)}, bf16[80,12800]{1,0:T(8,128)(2,1)}, u32[]{:S(2)}, u32[]{:S(2)}) collective-permute-start(bf16[80,12800]{1,0:T(8,128)(2,1)S(1)} %collective-permute-done.1), channel_id=1, source_target_pairs={{0,1},{1,2},{2,3},{3,4},{4,5},{5,6},{6,7},{7,0},{8,9},{9,10},{10,1... | collective-permute-start | bytes 6144008 | tf_op jit(solution)/shard_map/ppermute | solution.py:24
  154.4 220.7 %collective-permute-start.5 = (bf16[80,12800]{1,0:T(8,128)(2,1)}, bf16[80,12800]{1,0:T(8,128)(2,1)}, u32[]{:S(2)}, u32[]{:S(2)}) collective-permute-start(bf16[80,12800]{1,0:T(8,128)(2,1)} %collective-permute-done.4), channel_id=1, source_target_pairs={{0,7},{1,0},{2,1},{3,2},{4,3},{5,4},{6,5},{7,6},{8,15},{9,8},{10,9... | collective-permute-start | bytes 6144008 | tf_op jit(solution)/shard_map/ppermute | solution.py:26
  241.0 134.2 %collective-permute-start.3 = (bf16[80,12800]{1,0:T(8,128)(2,1)}, bf16[80,12800]{1,0:T(8,128)(2,1)}, u32[]{:S(2)}, u32[]{:S(2)}) collective-permute-start(bf16[80,12800]{1,0:T(8,128)(2,1)} %collective-permute-done.2), channel_id=1, source_target_pairs={{0,1},{1,2},{2,3},{3,4},{4,5},{5,6},{6,7},{7,0},{8,9},{9,10},{10,1... | collective-permute-start | bytes 6144008 | tf_op jit(solution)/shard_map/ppermute | solution.py:24
  243.6 591.7 %reduce-scatter.5.cloned.1.call-start = ((), (), s32[]{:S(2)}) async-start(), calls=%async_computation.6 | async-start | bytes 40960000 | tf_op jit(solution)/shard_map/reduce_scatter | solution.py:258
  374.1 7.5 copy-start.8
  375.1 7.9 copy-start.37
  375.1 7.9 copy-start.6
  375.1 82.3 %collective-permute-start.6 = (bf16[80,12800]{1,0:T(8,128)(2,1)}, bf16[80,12800]{1,0:T(8,128)(2,1)S(1)}, u32[]{:S(2)}, u32[]{:S(2)}) collective-permute-start(bf16[80,12800]{1,0:T(8,128)(2,1)} %collective-permute-done.5), channel_id=1, source_target_pairs={{0,7},{1,0},{2,1},{3,2},{4,3},{5,4},{6,5},{7,6},{8,15},{9,8},{10,9... | collective-permute-start | bytes 6144008 | tf_op jit(solution)/shard_map/ppermute | solution.py:26
  378.4 6.1 copy-start.2
  481.7 3.1 copy-start.18
  483.0 1.9 copy-start.20
  483.0 1.9 copy-start.28
  483.9 2.3 copy-start.1
  486.2 2.3 copy-start.30
  488.5 19.9 %copy-start.22 = (bf16[256,640]{1,0:T(8,128)(2,1)S(1)}, bf16[256,640]{1,0:T(8,128)(2,1)}, u32[]{:S(2)}) copy-start(bf16[256,640]{1,0:T(8,128)(2,1)} %param.17) | copy-start | bytes 983044
  506.9 1.5 copy-start.27
  544.0 6.2 copy-start.25
  544.1 7.4 copy-start.23
  550.6 0.8 copy-start.9
  551.6 0.7 copy-start.32
  556.5 3.7 copy-start.13
  556.5 3.7 copy-start.29
  556.5 7.8 slice-start
  560.3 14.4 copy-start.11
  560.3 4.1 slice-start.1
  564.4 1.4 copy-start.19
  564.4 2.5 copy-start.21
  565.8 1.7 copy-start.26
  566.9 7.8 copy-start.14
  567.6 7.1 copy-start.16
  567.6 6.7 copy-start.31
  567.6 6.7 copy-start.33
  599.6 384.7 %copy-start.45 = (s32[40]{0:T(128)S(1)}, s32[40]{0:T(128)}, u32[]{:S(2)}) copy-start(s32[40]{0:T(128)} %param.25) | copy-start | bytes 484
  599.6 384.7 %reduce-scatter.7.cloned.1.call-start = ((), (), s32[]{:S(2)}) async-start(), calls=%async_computation.7 | async-start | bytes 9216000 | tf_op jit(solution)/shard_map/reduce_scatter | solution.py:262
  835.3 183.4 %all-gather.7.cloned.1.call-start = ((), (), s32[]{:S(2)}) async-start(), calls=%async_computation.8 | async-start | bytes 5120000 | tf_op jit(solution)/shard_map/all_gather | solution.py:266
  1041.2 115.0 %all-to-all-start = ((f32[80,8,5,320]{3,0,2,1:T(8,128)}), f32[80,8,5,320]{3,0,2,1:T(8,128)}, u32[]{:S(2)}, u32[]{:S(2)}) async-start(f32[80,8,5,320]{3,0,2,1:T(8,128)} %bitcast.90), calls=%async_computation.3 | async-start | bytes 9830400 | tf_op jit(solution)/shard_map/all_to_all | solution.py:284
  1159.0 70.9 %slice-start.2 = ((s8[8192000]{0:T(1024)(128)(4,1)}), s8[4194304]{0:T(1024)(128)(4,1)S(1)}, s32[]{:S(2)}) async-start(s8[8192000]{0:T(1024)(128)(4,1)} %bitcast.88), calls=%async_computation.12 | async-start | bytes 8388608
  1192.4 37.6 %slice-start.3 = ((s8[8192000]{0:T(1024)(128)(4,1)}), s8[3997696]{0:T(1024)(128)(4,1)S(1)}, s32[]{:S(2)}) async-start(s8[8192000]{0:T(1024)(128)(4,1)} %bitcast.88), calls=%async_computation.13 | async-start | bytes 7995392
  1261.4 5.1 copy-start.42
  1261.4 5.1 copy-start.46
  1261.4 6.4 copy-start.44
  1261.4 232.8 %all-to-all-start.1 = ((f32[8,80,5,320]{3,1,2,0:T(8,128)}), f32[8,80,5,320]{3,1,2,0:T(8,128)}, u32[]{:S(2)}, u32[]{:S(2)}) async-start(f32[8,80,5,320]{3,1,2,0:T(8,128)} %copy.135), calls=%async_computation.4 | async-start | bytes 9830400 | tf_op jit(solution)/shard_map/all_to_all | solution.py:297
  1266.2 221.1 %reduce-scatter.9.cloned.1.call-start = ((), (), s32[]{:S(2)}) async-start(), calls=%async_computation.9 | async-start | bytes 368640 | tf_op jit(solution)/shard_map/reduce_scatter | solution.py:263
  1267.8 8.1 copy-start.41
  1267.8 8.3 copy-start.43
  1275.9 123.6 %copy-start.38 = (f32[256]{0:T(256)S(1)}, f32[256]{0:T(256)}, u32[]{:S(2)}) copy-start(f32[256]{0:T(256)} %copy-done.37) | copy-start | bytes 3076
  1275.9 125.8 %copy-start.12 = (bf16[20,32,256]{2,1,0:T(8,128)(2,1)S(1)}, bf16[20,32,256]{2,1,0:T(8,128)(2,1)}, u32[]{:S(2)}) copy-start(bf16[20,32,256]{2,1,0:T(8,128)(2,1)} %copy-done.11) | copy-start | bytes 983044
  1275.9 125.8 %copy-start.15 = (bf16[20,32,256]{2,1,0:T(8,128)(2,1)S(1)}, bf16[20,32,256]{2,1,0:T(8,128)(2,1)}, u32[]{:S(2)}) copy-start(bf16[20,32,256]{2,1,0:T(8,128)(2,1)} %copy-done.14) | copy-start | bytes 983044
  1396.2 5.5 copy-start.17
  1396.3 9.5 copy-start.10
  1396.3 9.5 copy-start.24
  1401.7 91.9 %copy-start.36 = (f32[80,16]{0,1:T(8,128)S(1)}, f32[80,16]{0,1:T(8,128)}, u32[]{:S(2)}) copy-start(f32[80,16]{0,1:T(8,128)} %param.22) | copy-start | bytes 15364
  1401.7 91.9 %copy-start.39 = (f32[80,16]{0,1:T(8,128)S(1)}, f32[80,16]{0,1:T(8,128)}, u32[]{:S(2)}) copy-start(f32[80,16]{0,1:T(8,128)} %param.23) | copy-start | bytes 15364
  1401.7 91.9 %copy-start.40 = (f32[80,16]{0,1:T(8,128)S(1)}, f32[80,16]{0,1:T(8,128)}, u32[]{:S(2)}) copy-start(f32[80,16]{0,1:T(8,128)} %param.24) | copy-start | bytes 15364
  1512.0 6.7 copy-start.3
  (1 other events, 0.7 us)
Sparse Core Ops, SparseCore 0:
  243.7 290.6 all-gather.4
  599.7 235.5 reduce-scatter.4
  839.0 145.2 reduce-scatter.6
  985.7 32.9 all-gather.6
  1425.7 61.5 reduce-scatter.8
